TPU v7x, 32 devices: a whole 2x2x4 slice. The times are simulated.
32 devices in a mesh: expert: 8 (over z, y), shard: 4 (over x, core).
Axes of the slice: x: 2, y: 2, z: 4, core: 2. Of those that a mesh axis runs over, the one named last changes fastest.
Arguments:
- tokens: float32 [25216, 512], P(('expert', 'shard')), may hold values from -6 to 6
- routes: int32 [25216, 2], P(('expert', 'shard')), may hold values from 0 to 7, all different within a row; in each aligned block of 394 rows (0 to 393, 394 to 787, ...) at most 192 rows name the same one
- priority: int32 [25216], P(('expert', 'shard')), may hold values from 0 to 393, as said below
- norm_gain: bfloat16 [2, 2, 512], P(None, None, 'shard'), may hold values from 0.5 to 1.5
- norm_bias: bfloat16 [2, 2, 512], P(None, None, 'shard'), may hold values from -1 to 1
- w_qkv: bfloat16 [2, 512, 1536], P(None, 'shard'), may hold values from -0.25 to 0.25
- w_proj: bfloat16 [2, 512, 512], P(None, 'shard'), may hold values from -2 to 2
- w_router: bfloat16 [2, 512, 8], P(None, 'shard'), may hold values from -0.1875 to 0.1875
- exp_in: bfloat16 [2, 8, 512, 2048], P(None, 'expert', 'shard'), may hold values from -0.25 to 0.25
- exp_out: bfloat16 [2, 8, 2048, 512], P(None, 'expert', 'shard'), may hold values from -0.875 to 0.875
- cotangent: float32 [25216, 512], P(('expert', 'shard')), may hold values from -6 to 6
Outputs:
- activations: float32 [25216, 512], P(('expert', 'shard'))
- d_tokens: float32 [25216, 512], P(('expert', 'shard'))
- grad_gain: float32 [2, 2, 512], P(None, None, 'shard')
- grad_bias: float32 [2, 2, 512], P(None, None, 'shard')
- grad_qkv: float32 [2, 512, 1536], P(None, 'shard')
- grad_proj: float32 [2, 512, 512], P(None, 'shard')
- grad_router: float32 [2, 512, 8], P(None, 'shard')
- grad_exp_in: float32 [2, 8, 512, 2048], P(None, 'expert', 'shard')
- grad_exp_out: float32 [2, 8, 2048, 512], P(None, 'expert', 'shard')
Inputs may be any that keep to these rules, and one draw needn't show every extreme that they name: `routes`: each row names 2 different experts; in each aligned block of 394 rows no expert is named by more than 192 rows. `priority`: in each aligned block of 394 rows the values are a permutation of 0 to 393.
All inputs are finite; a program needn't handle non-finite values.
Results may differ from a plain program's by a relative error of at most 0.025.
Values may be sent and summed in bfloat16 or wider, within the bound.
No kernel may reach another device: no remote copies, remote signals or barrier semaphores. Data moves between devices by JAX's collectives and lax.ppermute only.
A program may use at most 256 MiB of HBM per device.

v0:
```python
import jax
import jax.numpy as jnp
from jax import lax
from jax.sharding import PartitionSpec as P

D = 512
HEADS = 8
HEAD = 64
HIDDEN_SIZE = 2048
EXP_DEV = 1
SEQ = 197
MICRO = 2
LAYERS = 2
TOP = 2
TOK_MB = 394
norm_eps = 1e-06


def layer_norm(values, norm_scale, norm_shift):
    centre = values - jnp.mean(values, axis=-1, keepdims=True)
    spread = jnp.mean(centre * centre, axis=-1, keepdims=True)
    return centre * lax.rsqrt(spread + norm_eps) * norm_scale + norm_shift


def gelu_tanh(values):
    return jax.nn.gelu(values, approximate=True)


def dot_first(left, right):
    return lax.dot_general(
        left, right, (((0,), (0,)), ((), ())), preferred_element_type=jnp.float32
    )


def dot_last(left, right):
    return lax.dot_general(
        left, right, (((1,), (1,)), ((), ())), preferred_element_type=jnp.float32
    )


def slot_tables(route_ids, prio_rank, experts, capacity):
    tok_count = route_ids.shape[0]
    order_key = jnp.concatenate([prio_rank, prio_rank + tok_count])
    pair_expert = jnp.concatenate([route_ids[:, 0], route_ids[:, 1]])
    same_expert = pair_expert[:, None] == pair_expert[None, :]
    earlier = order_key[None, :] < order_key[:, None]
    position = jnp.sum((same_expert & earlier).astype(jnp.int32), axis=1)
    kept_mask = position < capacity
    flat_slot = jnp.where(kept_mask, pair_expert * capacity + position, experts * capacity)
    pair_ids = jnp.arange(2 * tok_count, dtype=jnp.int32)
    slot_pair = (
        jnp.full((experts * capacity + 1,), 2 * tok_count, jnp.int32).at[flat_slot].set(pair_ids)
    )
    slot_pair = slot_pair[: experts * capacity]
    slot_token = jnp.where(slot_pair < 2 * tok_count, slot_pair % tok_count, tok_count)
    return (flat_slot, slot_pair, slot_token, kept_mask)


def block_tables(route_ids, prio_rank, experts, capacity):
    blocks, tok_count = prio_rank.shape
    flat_slot, slot_pair, slot_token, kept_mask = jax.vmap(
        lambda r, p: slot_tables(r, p, experts, capacity)
    )(route_ids, prio_rank)
    block_ids = jnp.arange(blocks, dtype=jnp.int32)
    send_index = (
        (block_ids[:, None] * (tok_count + 1) + slot_token)
        .reshape(blocks, experts, capacity)
        .transpose(1, 0, 2)
    )
    pair_index = (
        (block_ids[:, None] * (2 * tok_count + 1) + slot_pair)
        .reshape(blocks, experts, capacity)
        .transpose(1, 0, 2)
    )
    slot_e = flat_slot // capacity
    slot_c = flat_slot % capacity
    back_index = jnp.where(
        kept_mask,
        (slot_e * blocks + block_ids[:, None]) * capacity + slot_c,
        experts * blocks * capacity,
    )
    return (send_index, pair_index, back_index, kept_mask)


def forward_layer(residual, route_hot, tables, weights, experts, capacity):
    norm_gains, norm_shifts, qkv_w, proj_w, router_w, in_w, out_w = weights
    send_index, pair_index, back_index, kept_mask = tables
    tok_count = residual.shape[0]
    blocks = back_index.shape[0]
    tok_block = tok_count // blocks
    seq_count = tok_count // SEQ
    score_scale = HEAD ** (-0.5)
    norm_scale = norm_gains.astype(jnp.float32)
    norm_shift = norm_shifts.astype(jnp.float32)
    normed = layer_norm(residual, norm_scale[0], norm_shift[0]).astype(jnp.bfloat16)
    qkv_rows = jnp.dot(normed, qkv_w, preferred_element_type=jnp.float32).astype(jnp.bfloat16)
    heads = qkv_rows.reshape(seq_count, SEQ, 3, HEADS, HEAD)
    scores = (
        jnp.einsum(
            "sqhd,skhd->shqk", heads[:, :, 0], heads[:, :, 1], preferred_element_type=jnp.float32
        )
        * score_scale
    )
    row_top = jnp.max(scores, axis=-1, keepdims=True)
    scores_exp = jnp.exp(scores - row_top)
    row_total = jnp.sum(scores_exp, axis=-1, keepdims=True)
    soft_scores = scores_exp / row_total
    log_total = row_top + jnp.log(row_total)
    mixed_heads = jnp.einsum(
        "shqk,skhd->sqhd",
        soft_scores.astype(jnp.bfloat16),
        heads[:, :, 2],
        preferred_element_type=jnp.float32,
    )
    mixed_heads = mixed_heads.astype(jnp.bfloat16).reshape(tok_count, D)
    middle = residual + jnp.dot(mixed_heads, proj_w, preferred_element_type=jnp.float32)
    normed_two = layer_norm(middle, norm_scale[1], norm_shift[1]).astype(jnp.bfloat16)
    gate_probs = jax.nn.softmax(
        jnp.dot(normed_two, router_w, preferred_element_type=jnp.float32), axis=-1
    )
    padded = jnp.concatenate(
        [normed_two.reshape(blocks, tok_block, D), jnp.zeros((blocks, 1, D), jnp.bfloat16)], axis=1
    ).reshape(blocks * (tok_block + 1), D)
    sending = padded[send_index]
    received = lax.all_to_all(sending, "expert", split_axis=0, concat_axis=0, tiled=True)
    row_block = received.reshape(experts * blocks * capacity, D)
    hidden_pre = jnp.dot(row_block, in_w[0], preferred_element_type=jnp.float32)
    hidden_act = gelu_tanh(hidden_pre).astype(jnp.bfloat16)
    expert_rows = jnp.dot(hidden_act, out_w[0], preferred_element_type=jnp.float32).astype(
        jnp.bfloat16
    )
    returned = lax.all_to_all(
        expert_rows.reshape(experts, blocks, capacity, D),
        "expert",
        split_axis=0,
        concat_axis=0,
        tiled=True,
    )
    back_rows = jnp.concatenate(
        [returned.reshape(experts * blocks * capacity, D), jnp.zeros((1, D), jnp.bfloat16)]
    )
    pair_rows = back_rows[back_index].astype(jnp.float32).reshape(blocks, TOP, tok_block, D)
    probs_block = gate_probs.reshape(blocks, tok_block, experts)
    chosen = jnp.sum(route_hot * probs_block[:, :, None, :], axis=-1)
    kept_gate = kept_mask.astype(jnp.float32).reshape(blocks, TOP, tok_block)
    weight_pair = kept_gate * chosen.transpose(0, 2, 1)
    combined = jnp.sum(weight_pair[..., None] * pair_rows, axis=1)
    output = middle + combined.reshape(tok_count, D)
    saved_state = (
        residual,
        normed,
        heads,
        log_total,
        mixed_heads,
        middle,
        normed_two,
        gate_probs,
        kept_gate,
        weight_pair,
        pair_rows,
        row_block,
        hidden_pre,
    )
    return (output, saved_state)


def backward_layer(d_output, saved_state, route_hot, tables, weights, experts, capacity):
    (
        residual,
        normed,
        heads,
        log_total,
        mixed_heads,
        middle,
        normed_two,
        gate_probs,
        kept_gate,
        weight_pair,
        pair_rows,
        row_block,
        hidden_pre,
    ) = saved_state
    send_index, pair_index, back_index, kept_mask = tables
    norm_gains, norm_shifts, qkv_w, proj_w, router_w, in_w, out_w = weights
    tok_count = residual.shape[0]
    blocks = back_index.shape[0]
    tok_block = tok_count // blocks
    seq_count = tok_count // SEQ
    score_scale = HEAD ** (-0.5)
    norm_scale = norm_gains.astype(jnp.float32)
    norm_shift = norm_shifts.astype(jnp.float32)
    d_block = d_output.reshape(blocks, 1, tok_block, D)
    d_gate_pair = kept_gate * jnp.sum(d_block * pair_rows, axis=-1)
    d_gates = jnp.sum(route_hot * d_gate_pair.transpose(0, 2, 1)[..., None], axis=2)
    d_gates = d_gates.reshape(tok_count, experts)
    d_logits = (
        gate_probs * (d_gates - jnp.sum(gate_probs * d_gates, axis=-1, keepdims=True))
    ).astype(jnp.bfloat16)
    g_router = dot_first(normed_two, d_logits)
    d_normed_two = dot_last(d_logits, router_w)
    d_pairs = (
        (weight_pair[..., None] * d_block).astype(jnp.bfloat16).reshape(blocks, TOP * tok_block, D)
    )
    d_pairs = jnp.concatenate([d_pairs, jnp.zeros((blocks, 1, D), jnp.bfloat16)], axis=1).reshape(
        blocks * (TOP * tok_block + 1), D
    )
    d_slots = d_pairs[pair_index]
    d_expert_out = lax.all_to_all(d_slots, "expert", split_axis=0, concat_axis=0, tiled=True)
    flat_out = d_expert_out.reshape(experts * blocks * capacity, D)
    hidden_act = gelu_tanh(hidden_pre).astype(jnp.bfloat16)
    g_out = dot_first(hidden_act, flat_out)
    d_act = dot_last(flat_out, out_w[0])
    d_pre = jax.vjp(gelu_tanh, hidden_pre)[1](d_act)[0].astype(jnp.bfloat16)
    g_in = dot_first(row_block, d_pre)
    d_rows = dot_last(d_pre, in_w[0]).astype(jnp.bfloat16).reshape(experts, blocks, capacity, D)
    d_back = lax.all_to_all(d_rows, "expert", split_axis=0, concat_axis=0, tiled=True)
    d_pair_in = jnp.concatenate(
        [d_back.reshape(experts * blocks * capacity, D), jnp.zeros((1, D), jnp.bfloat16)]
    )[back_index]
    d_pair_in = d_pair_in.astype(jnp.float32).reshape(blocks, TOP, tok_block, D)
    d_normed_two = d_normed_two + jnp.sum(d_pair_in, axis=1).reshape(tok_count, D)
    pulled_two = jax.vjp(layer_norm, middle, norm_scale[1], norm_shift[1])[1](d_normed_two)
    d_middle = d_output + pulled_two[0]
    d_branch = d_middle.astype(jnp.bfloat16)
    g_proj = dot_first(mixed_heads, d_branch)
    d_mixed = dot_last(d_branch, proj_w).astype(jnp.bfloat16).reshape(seq_count, SEQ, HEADS, HEAD)
    query_heads = heads[:, :, 0]
    key_heads = heads[:, :, 1]
    value_heads = heads[:, :, 2]
    scores = (
        jnp.einsum("sqhd,skhd->shqk", query_heads, key_heads, preferred_element_type=jnp.float32)
        * score_scale
    )
    soft_scores = jnp.exp(scores - log_total)
    d_soft = jnp.einsum("sqhd,skhd->shqk", d_mixed, value_heads, preferred_element_type=jnp.float32)
    d_values = jnp.einsum(
        "shqk,sqhd->skhd",
        soft_scores.astype(jnp.bfloat16),
        d_mixed,
        preferred_element_type=jnp.float32,
    )
    d_scores = (
        soft_scores * (d_soft - jnp.sum(soft_scores * d_soft, axis=-1, keepdims=True))
    ).astype(jnp.bfloat16)
    d_query = (
        jnp.einsum("shqk,skhd->sqhd", d_scores, key_heads, preferred_element_type=jnp.float32)
        * score_scale
    )
    d_keys = (
        jnp.einsum("shqk,sqhd->skhd", d_scores, query_heads, preferred_element_type=jnp.float32)
        * score_scale
    )
    d_qkv = (
        jnp.stack([d_query, d_keys, d_values], axis=2)
        .reshape(tok_count, 3 * D)
        .astype(jnp.bfloat16)
    )
    g_qkv = dot_first(normed, d_qkv)
    d_normed = dot_last(d_qkv, qkv_w)
    pulled_one = jax.vjp(layer_norm, residual, norm_scale[0], norm_shift[0])[1](d_normed)
    d_residual = d_middle + pulled_one[0]
    g_gain = jnp.stack([pulled_one[1], pulled_two[1]])
    g_shift = jnp.stack([pulled_one[2], pulled_two[2]])
    return (d_residual, (g_gain, g_shift, g_qkv, g_proj, g_router, g_in[None], g_out[None]))


SCATTER_DIMS = (1, 1, 0, 0, 0, 1, 1)


def reduce_layer(layer_grads):
    scattered = [
        lax.psum_scatter(
            grad.astype(jnp.bfloat16), "shard", scatter_dimension=dim, tiled=True
        ).astype(jnp.float32)
        for grad, dim in zip(layer_grads, SCATTER_DIMS)
    ]
    replicated = [
        lax.psum(part.astype(jnp.bfloat16), "expert").astype(jnp.float32) for part in scattered[:5]
    ]
    return replicated + scattered[5:]


def local(
    tokens,
    routes,
    priority,
    norm_gain,
    norm_bias,
    w_qkv,
    w_proj,
    w_router,
    exp_in,
    exp_out,
    cotangent,
):
    experts = lax.axis_size("expert") * EXP_DEV
    capacity = max(8, (5 * TOK_MB // (2 * experts) + 7) // 8 * 8)
    tok_count = tokens.shape[0]
    blocks = tok_count // TOK_MB
    route_ids = routes.reshape(blocks, TOK_MB, TOP)
    prio_rank = priority.reshape(blocks, TOK_MB)
    tables = block_tables(route_ids, prio_rank, experts, capacity)
    route_hot = (route_ids[..., None] == jnp.arange(experts, dtype=jnp.int32)).astype(jnp.float32)
    all_weights = []
    for layer_index in range(LAYERS):
        all_weights.append(
            (
                lax.all_gather(norm_gain[layer_index], "shard", axis=1, tiled=True),
                lax.all_gather(norm_bias[layer_index], "shard", axis=1, tiled=True),
                lax.all_gather(w_qkv[layer_index], "shard", axis=0, tiled=True),
                lax.all_gather(w_proj[layer_index], "shard", axis=0, tiled=True),
                lax.all_gather(w_router[layer_index], "shard", axis=0, tiled=True),
                lax.all_gather(exp_in[layer_index], "shard", axis=1, tiled=True),
                lax.all_gather(exp_out[layer_index], "shard", axis=1, tiled=True),
            )
        )
    residual = tokens
    saved_list = []
    for layer_index in range(LAYERS):
        residual, saved_state = forward_layer(
            residual, route_hot, tables, all_weights[layer_index], experts, capacity
        )
        saved_list.append(saved_state)
    activations = residual
    d_residual = cotangent
    reduced = [None] * LAYERS
    for layer_index in reversed(range(LAYERS)):
        d_residual, layer_grads = backward_layer(
            d_residual,
            saved_list[layer_index],
            route_hot,
            tables,
            all_weights[layer_index],
            experts,
            capacity,
        )
        reduced[layer_index] = reduce_layer(layer_grads)
    outs = [jnp.stack([reduced[l][k] for l in range(LAYERS)]) for k in range(7)]
    return (activations, d_residual, *outs)


def solution(mesh):
    return jax.shard_map(
        local,
        mesh=mesh,
        in_specs=(
            P(("expert", "shard"), None),
            P(("expert", "shard"), None),
            P(("expert", "shard")),
            P(None, None, "shard"),
            P(None, None, "shard"),
            P(None, "shard", None),
            P(None, "shard", None),
            P(None, "shard", None),
            P(None, "expert", "shard", None),
            P(None, "expert", "shard", None),
            P(("expert", "shard"), None),
        ),
        out_specs=(
            P(("expert", "shard"), None),
            P(("expert", "shard"), None),
            P(None, None, "shard"),
            P(None, None, "shard"),
            P(None, "shard", None),
            P(None, "shard", None),
            P(None, "shard", None),
            P(None, "expert", "shard", None),
            P(None, "expert", "shard", None),
        ),
        check_vma=False,
    )
```

profile of v0, /device:TPU:0, one launch (start us, length us, event | category | flops | bytes accessed | tf_op | source)
XLA Modules:
  0.0 1172.4 jit_solution(14263850944963940253)
XLA Ops:
  10.7 6.0 all-gather.1
  16.7 5.4 all-gather
  24.2 16.5 %fusion.16 = s32[2,788]{0,1:T(8,128)S(1)} fusion(s32[2,788]{0,1:T(8,128)S(1)} %copy.267, s32[2,788]{1,0:T(2,128)S(1)} %get-tuple-element.105, s32[2,788]{1,0:T(2,128)S(1)} %get-tuple-element.104, s32[2,788]{0,1:T(8,128)S(1)} %copy.266), kind=kLoop, calls=%fused_computation.42 | loop fusion | flops 6207864 | bytes 31520 | tf_op jit(solution)/shard_map/vmap()/reduce_sum | solution.py:47
  44.0 8.8 scatter_custom_fusion
  53.0 8.3 all-gather.3
  65.7 7.2 reshape.713
  98.6 9.2 gather_fusion
  107.8 6.1 all-to-all-start
  115.2 47.6 %all-to-all-done = bf16[8,2,128,512]{3,2,1,0:T(8,128)(2,1)} async-done(((bf16[8,2,128,512]{3,2,1,0:T(8,128)(2,1)}), bf16[8,2,128,512]{3,2,1,0:T(8,128)(2,1)}, u32[]{:S(2)}, u32[]{:S(2)}) %all-to-all-start) | async-done | bytes 2097184 | tf_op jit(solution)/shard_map/all_to_all | solution.py:125
  162.8 14.2 %multiply_convert_fusion.1 = (bf16[2048,2048]{1,0:T(8,128)(2,1)}, f32[2048,2048]{1,0:T(8,128)}) fusion(bf16[2048,512]{1,0:T(8,128)(2,1)} %bitcast.20, bf16[1,1,512,2048]{3,2,1,0:T(8,128)(2,1)} %all-gather.23.cloned.1.call-done), kind=kOutput, calls=%fused_computation.28 | convolution fusion | flops 4332716032 | bytes 29360128 | tf_op jit(solution)/shard_map/dot_general | solution.py:127
  176.9 9.8 convolution_convert_fusion.11
  192.5 5.1 all-gather.8
  197.5 5.0 all-gather.7
  202.6 5.3 all-gather.4
  207.9 9.0 all-gather.10
  218.7 20.5 %all-to-all-done.1 = bf16[8,2,128,512]{3,2,1,0:T(8,128)(2,1)} async-done(((bf16[8,2,128,512]{3,2,1,0:T(8,128)(2,1)}), bf16[8,2,128,512]{3,2,1,0:T(8,128)(2,1)}, u32[]{:S(2)}, u32[]{:S(2)}) %all-to-all-start.1) | async-done | bytes 2097184 | tf_op jit(solution)/shard_map/all_to_all | solution.py:132
  240.9 6.4 gather_fusion.1
  261.7 7.2 reshape.714
  294.1 9.2 gather_fusion.2
  315.3 5.2 all-gather.11
  323.8 9.2 gather_fusion.4
  333.0 22.5 %all-to-all-done.2 = bf16[8,2,128,512]{3,2,1,0:T(8,128)(2,1)} async-done(((bf16[8,2,128,512]{3,2,1,0:T(8,128)(2,1)}), bf16[8,2,128,512]{3,2,1,0:T(8,128)(2,1)}, u32[]{:S(2)}, u32[]{:S(2)}) %all-to-all-start.2) | async-done | bytes 2097184 | tf_op jit(solution)/shard_map/all_to_all | solution.py:125
  359.7 14.4 %multiply_convert_fusion = (bf16[2048,2048]{1,0:T(8,128)(2,1)}, f32[2048,2048]{1,0:T(8,128)}) fusion(bf16[2048,512]{1,0:T(8,128)(2,1)} %bitcast.38, bf16[1,1,512,2048]{3,2,1,0:T(8,128)(2,1)} %all-gather.29.cloned.1.call-done), kind=kOutput, calls=%fused_computation.27 | convolution fusion | flops 4332716032 | bytes 29360128 | tf_op jit(solution)/shard_map/dot_general | solution.py:127
  374.1 11.0 all-gather.31.cloned.1.call-done
  385.1 22.4 %all-to-all-done.4 = bf16[8,2,128,512]{3,2,1,0:T(8,128)(2,1)S(1)} async-done(((bf16[8,2,128,512]{3,2,1,0:T(8,128)(2,1)}), bf16[8,2,128,512]{3,2,1,0:T(8,128)(2,1)S(1)}, u32[]{:S(2)}, u32[]{:S(2)}) %all-to-all-start.4) | async-done | bytes 2097184 | tf_op jit(solution)/shard_map/all_to_all | solution.py:208
  407.5 17.1 %fusion.13 = bf16[2048,2048]{1,0:T(8,128)(2,1)S(1)} fusion(f32[2048,2048]{1,0:T(8,128)} %get-tuple-element.95, bf16[2048,512]{1,0:T(8,128)(2,1)S(1)} %bitcast.301, bf16[1,1,2048,512]{3,2,1,0:T(8,128)(2,1)} %all-gather.31.cloned.1.call-done), kind=kOutput, calls=%fused_computation.26 | convolution fusion | flops 4378853376 | bytes 29360128 | tf_op jit(solution)/shard_map/dot_general | solution.py:36
  424.7 6.1 convolution_convert_fusion.9
  434.3 9.8 convolution_convert_fusion.10
  444.2 38.6 %all-to-all-done.5 = bf16[8,2,128,512]{3,2,1,0:T(8,128)(2,1)S(1)} async-done(((bf16[8,2,128,512]{3,2,1,0:T(8,128)(2,1)}), bf16[8,2,128,512]{3,2,1,0:T(8,128)(2,1)S(1)}, u32[]{:S(2)}, u32[]{:S(2)}) %all-to-all-start.5) | async-done | bytes 2097184 | tf_op jit(solution)/shard_map/all_to_all | solution.py:216
  484.1 4.6 all-to-all-start.3
  490.5 6.0 gather_fusion.5
  496.5 39.9 %all-to-all-done.3 = bf16[8,2,128,512]{3,2,1,0:T(8,128)(2,1)} async-done(((bf16[8,2,128,512]{3,2,1,0:T(8,128)(2,1)}), bf16[8,2,128,512]{3,2,1,0:T(8,128)(2,1)}, u32[]{:S(2)}, u32[]{:S(2)}) %all-to-all-start.3) | async-done | bytes 2097184 | tf_op jit(solution)/shard_map/all_to_all | solution.py:132
  538.2 6.0 gather_fusion.3
  571.6 4.5 multiply_reduce_fusion.1
  583.3 4.5 copy.292
  587.8 7.0 convert_element_type.280
  609.2 9.2 gather_fusion.6
  618.4 52.1 %all_to_all.40 = bf16[8,2,128,512]{3,2,1,0:T(8,128)(2,1)S(1)} all-to-all(bf16[8,2,128,512]{3,2,1,0:T(8,128)(2,1)} %bitcast.299), channel_id=1, replica_groups=mesh['expert'=8,'shard'=4] {'expert'}, dimensions={0} | all-to-all | bytes 4194304 | tf_op jit(solution)/shard_map/all_to_all | solution.py:208
  670.5 17.5 %fusion.6 = bf16[2048,2048]{1,0:T(8,128)(2,1)S(1)} fusion(f32[2048,2048]{1,0:T(8,128)} %get-tuple-element.85, bf16[2048,512]{1,0:T(8,128)(2,1)S(1)} %bitcast.303, bf16[1,1,2048,512]{3,2,1,0:T(8,128)(2,1)S(1)} %copy-done.103), kind=kOutput, calls=%fused_computation.19 | convolution fusion | flops 4378853376 | bytes 29360128 | tf_op jit(solution)/shard_map/dot_general | solution.py:36
  688.0 6.1 convolution_convert_fusion.8
  694.1 4.6 all-to-all-start.7
  709.2 5.2 convolution_convert_fusion.6
  714.5 31.5 %all-to-all-done.7 = bf16[8,2,128,512]{3,2,1,0:T(8,128)(2,1)} async-done(((bf16[8,2,128,512]{3,2,1,0:T(8,128)(2,1)}), bf16[8,2,128,512]{3,2,1,0:T(8,128)(2,1)}, u32[]{:S(2)}, u32[]{:S(2)}) %all-to-all-start.7) | async-done | bytes 2097184 | tf_op jit(solution)/shard_map/all_to_all | solution.py:216
  747.7 6.0 gather_fusion.7
  771.0 5.3 fusion.57
  776.3 4.5 multiply_reduce_fusion
  781.3 6.4 multiply_convert_fusion.2
  795.3 6.9 convert_element_type.291
  802.3 5.3 convolution_convert_fusion.7
  807.7 4.9 multiply_reduce_fusion.11
  814.6 9.9 fusion.32
  824.5 10.1 fusion.31
  834.8 9.9 fusion.30
  844.8 9.9 fusion.29
  861.5 7.6 reduce-scatter.31.cloned.1.call-done
  869.1 30.4 %reduce-scatter.27.cloned.1.call-done = bf16[128,1536]{1,0:T(8,128)(2,1)} async-done(((bf16[512,1536]{1,0:T(8,128)(2,1)}), bf16[128,1536]{1,0:T(8,128)(2,1)}) %reduce-scatter.27.cloned.1.call-update) | async-done | bytes 393232 | tf_op jit(solution)/shard_map/reduce_scatter | solution.py:272
  902.3 19.1 %reduce-scatter.47.cloned.1.call-done = bf16[128,2]{1,0:T(8,128)(2,1)} async-done(((bf16[512,2]{1,0:T(8,128)(2,1)}), bf16[128,2]{1,0:T(8,128)(2,1)}) %reduce-scatter.47.cloned.1.call-update) | async-done | bytes 528
  922.2 21.1 %reduce-scatter.43.cloned.1.call-done = bf16[128,2]{1,0:T(8,128)(2,1)} async-done(((bf16[512,2]{1,0:T(8,128)(2,1)}), bf16[128,2]{1,0:T(8,128)(2,1)}) %reduce-scatter.43.cloned.1.call-update) | async-done | bytes 528
  944.2 21.6 %all-reduce.8 = (bf16[1,2,128]{2,1,0:T(2,128)(2,1)S(1)}, bf16[1,2,128]{2,1,0:T(2,128)(2,1)S(1)}, bf16[1,2,128]{2,1,0:T(2,128)(2,1)S(1)}, bf16[1,2,128]{2,1,0:T(2...) all-reduce(bf16[1,2,128]{2,1,0:T(2,128)(2,1)S(1)} %bitcast.346, ...), channel_id=1, replica_groups=mesh['expert'=8,'shard'=4] {'expert'}, use_global_device_ids=true, to_apply=%region_47.48 | all-reduce | flops 3072 | bytes 12288 | tf_op jit(solution)/shard_map/psum | solution.py:278
  967.6 9.9 reduce-scatter.41.cloned.1.call-done
  977.5 33.6 %reduce-scatter.39.cloned.1.call-done = bf16[1,512,512]{2,1,0:T(8,128)(2,1)} async-done(((bf16[1,2048,512]{2,1,0:T(8,128)(2,1)}), bf16[1,512,512]{2,1,0:T(8,128)(2,1)}) %reduce-scatter.39.cloned.1.call-update) | async-done | bytes 524304 | tf_op jit(solution)/shard_map/reduce_scatter | solution.py:272
  1013.8 31.7 %reduce-scatter.37.cloned.1.call-done = bf16[1,128,2048]{2,1,0:T(8,128)(2,1)} async-done(((bf16[1,512,2048]{2,1,0:T(8,128)(2,1)}), bf16[1,128,2048]{2,1,0:T(8,128)(2,1)}) %reduce-scatter.37.cloned.1.call-update) | async-done | bytes 524304 | tf_op jit(solution)/shard_map/reduce_scatter | solution.py:272
  1045.4 33.6 %reduce-scatter.35.cloned.1.call-done = bf16[1,128,2048]{2,1,0:T(8,128)(2,1)} async-done(((bf16[1,512,2048]{2,1,0:T(8,128)(2,1)}), bf16[1,128,2048]{2,1,0:T(8,128)(2,1)}) %reduce-scatter.35.cloned.1.call-update) | async-done | bytes 524304 | tf_op jit(solution)/shard_map/reduce_scatter | solution.py:272
  1081.7 79.5 %all-reduce.12.cloned.1.call-done = (bf16[1,128,1536]{2,1,0:T(8,128)(2,1)}, bf16[1,128,1536]{2,1,0:T(8,128)(2,1)}, bf16[1,128,512]{2,1,0:T(8,128)(2,1)}, bf16[1,128,512]{2,1,0:T(8,128)(2,1)}) async-done(((bf16[1,128,1536]{2,1,0:T(8,128)(2,1)}, bf16[1,128,1536]{2,1,0:T(8,128)(2,1)}, bf16[1,128,512]{2,1,0:T(8,128)(2,1)}, bf16[1,128,512]{2,1,0:T(8,128)(2,1)}), (bf16[1,128,1536]{2,1,0:T(8,128)(2,1)}, ...) | async-done | bytes 1048592 | tf_op jit(solution)/shard_map/psum | solution.py:278
  (501 shorter events, 226.9 us)
Async XLA Ops:
  7.2 14.9 %copy-start.92 = (s32[788]{0:T(1024)S(1)}, s32[788]{0:T(1024)}, u32[]{:S(2)}) copy-start(s32[788]{0:T(1024)} %param.13) | copy-start | bytes 9460
  7.2 15.0 %copy-start.9 = (f32[788,512]{1,0:T(8,128)S(1)}, f32[788,512]{1,0:T(8,128)}, u32[]{:S(2)}) copy-start(f32[788,512]{1,0:T(8,128)} %param.11) | copy-start | bytes 4841476
  7.2 54.0 %all-gather.21.cloned.1.call-start = ((), (), s32[]{:S(2)}) async-start(), calls=%async_computation.30 | async-start | bytes 1966080 | tf_op jit(solution)/shard_map/all_gather | solution.py:310
  9.5 105.7 %all-gather.23.cloned.1.call-start = ((), (), s32[]{:S(2)}) async-start(), calls=%async_computation.31 | async-start | bytes 2621440 | tf_op jit(solution)/shard_map/all_gather | solution.py:313
  10.6 12.3 %copy-start.91 = (s32[788,2]{0,1:T(2,128)S(1)}, s32[788,2]{0,1:T(2,128)}, u32[]{:S(2)}) copy-start(s32[788,2]{0,1:T(2,128)} %param.12) | copy-start | bytes 18916
  10.6 12.4 %copy-start.58 = (bf16[2,128,512]{2,1,0:T(8,128)(2,1)S(1)}, bf16[2,128,512]{2,1,0:T(8,128)(2,1)}, u32[]{:S(2)}) copy-start(bf16[2,128,512]{2,1,0:T(8,128)(2,1)} %param.17) | copy-start | bytes 786436
  22.1 39.2 %copy-start.87 = (f32[1,1,512]{2,1,0:T(1,128)}, f32[1,1,512]{2,1,0:T(1,128)S(1)}, u32[]{:S(2)}) copy-start(f32[1,1,512]{2,1,0:T(1,128)S(1)} %get-tuple-element.73) | copy-start | bytes 6148
  22.1 75.0 %copy-start.81 = (f32[1,1,512]{2,1,0:T(1,128)}, f32[1,1,512]{2,1,0:T(1,128)S(1)}, u32[]{:S(2)}) copy-start(f32[1,1,512]{2,1,0:T(1,128)S(1)} %get-tuple-element.72) | copy-start | bytes 6148
  22.1 39.1 %copy-start.94 = (f32[1,1,512]{2,1,0:T(1,128)}, f32[1,1,512]{2,1,0:T(1,128)S(1)}, u32[]{:S(2)}) copy-start(f32[1,1,512]{2,1,0:T(1,128)S(1)} %get-tuple-element.75) | copy-start | bytes 6148
  22.4 38.8 %copy-start.77 = (f32[788]{0:T(1024)}, f32[788]{0:T(1024)S(1)}, u32[]{:S(2)}) copy-start(f32[788]{0:T(1024)S(1)} %broadcast_multiply_fusion.3) | copy-start | bytes 9460
  22.8 38.4 %copy-start.83 = (f32[788]{0:T(1024)}, f32[788]{0:T(1024)S(1)}, u32[]{:S(2)}) copy-start(f32[788]{0:T(1024)S(1)} %fusion.115) | copy-start | bytes 9460
  23.7 19.3 %copy-start.101 = (s32[2]{0:T(128)S(1)}, s32[2]{0:T(128)}, u32[]{:S(2)}) copy-start(s32[2]{0:T(128)} %constant.144) | copy-start | bytes 28
  23.7 19.4 %copy-start.100 = (s32[2]{0:T(128)S(1)}, s32[2]{0:T(128)}, u32[]{:S(2)}) copy-start(s32[2]{0:T(128)} %constant.141) | copy-start | bytes 28
  98.2 118.8 %copy-start.24 = (bf16[788,512]{1,0:T(8,128)(2,1)}, bf16[788,512]{1,0:T(8,128)(2,1)S(1)}, u32[]{:S(2)}) copy-start(bf16[788,512]{1,0:T(8,128)(2,1)S(1)} %add_convert_fusion.2) | copy-start | bytes 2420740
  107.8 54.9 %all-to-all-start = ((bf16[8,2,128,512]{3,2,1,0:T(8,128)(2,1)}), bf16[8,2,128,512]{3,2,1,0:T(8,128)(2,1)}, u32[]{:S(2)}, u32[]{:S(2)}) async-start(bf16[8,2,128,512]{3,2,1,0:T(8,128)(2,1)} %bitcast.298), calls=%async_computation | async-start | bytes 4194304 | tf_op jit(solution)/shard_map/all_to_all | solution.py:125
  113.9 63.0 %all-gather.25.cloned.1.call-start = ((), (), s32[]{:S(2)}) async-start(), calls=%async_computation.32 | async-start | bytes 2621440 | tf_op jit(solution)/shard_map/all_gather | solution.py:314
  186.8 15.8 %copy-start.93 = (bf16[2,128,8]{1,2,0:T(8,128)(2,1)S(1)}, bf16[2,128,8]{1,2,0:T(8,128)(2,1)}, u32[]{:S(2)}) copy-start(bf16[2,128,8]{1,2,0:T(8,128)(2,1)} %param.18) | copy-start | bytes 12292
  186.8 52.4 %all-to-all-start.1 = ((bf16[8,2,128,512]{3,2,1,0:T(8,128)(2,1)}), bf16[8,2,128,512]{3,2,1,0:T(8,128)(2,1)}, u32[]{:S(2)}, u32[]{:S(2)}) async-start(bf16[8,2,128,512]{3,2,1,0:T(8,128)(2,1)} %bitcast.306), calls=%async_computation.1 | async-start | bytes 4194304 | tf_op jit(solution)/shard_map/all_to_all | solution.py:132
  191.2 66.0 %all-gather.27.cloned.1.call-start = ((), (), s32[]{:S(2)}) async-start(), calls=%async_computation.33 | async-start | bytes 1966080 | tf_op jit(solution)/shard_map/all_gather | solution.py:310
  207.9 32.9 %copy-start.65 = (bf16[1,512,8]{1,2,0:T(8,128)(2,1)}, bf16[1,512,8]{1,2,0:T(8,128)(2,1)S(1)}, u32[]{:S(2)}) copy-start(bf16[1,512,8]{1,2,0:T(8,128)(2,1)S(1)} %all-gather.4) | copy-start | bytes 24580
  216.9 40.3 %copy-start.89 = (f32[1,1,512]{2,1,0:T(1,128)}, f32[1,1,512]{2,1,0:T(1,128)S(1)}, u32[]{:S(2)}) copy-start(f32[1,1,512]{2,1,0:T(1,128)S(1)} %get-tuple-element.69) | copy-start | bytes 6148
  217.0 40.3 %copy-start.96 = (f32[1,1,512]{2,1,0:T(1,128)}, f32[1,1,512]{2,1,0:T(1,128)S(1)}, u32[]{:S(2)}) copy-start(f32[1,1,512]{2,1,0:T(1,128)S(1)} %get-tuple-element.71) | copy-start | bytes 6148
  217.3 23.6 %copy-start.61 = (f32[788]{0:T(1024)}, f32[788]{0:T(1024)S(1)}, u32[]{:S(2)}) copy-start(f32[788]{0:T(1024)S(1)} %get-tuple-element.86) | copy-start | bytes 9460
  256.8 34.4 %copy-start.11 = (f32[788,512]{1,0:T(8,128)}, f32[788,512]{1,0:T(8,128)S(1)}, u32[]{:S(2)}) copy-start(f32[788,512]{1,0:T(8,128)S(1)} %get-tuple-element.42) | copy-start | bytes 4841476
  293.6 26.8 %copy-start.25 = (bf16[788,512]{1,0:T(8,128)(2,1)}, bf16[788,512]{1,0:T(8,128)(2,1)S(1)}, u32[]{:S(2)}) copy-start(bf16[788,512]{1,0:T(8,128)(2,1)S(1)} %add_convert_fusion) | copy-start | bytes 2420740
  303.3 52.2 %all-to-all-start.2 = ((bf16[8,2,128,512]{3,2,1,0:T(8,128)(2,1)}), bf16[8,2,128,512]{3,2,1,0:T(8,128)(2,1)}, u32[]{:S(2)}, u32[]{:S(2)}) async-start(bf16[8,2,128,512]{3,2,1,0:T(8,128)(2,1)} %bitcast.296), calls=%async_computation.2 | async-start | bytes 4194304 | tf_op jit(solution)/shard_map/all_to_all | solution.py:125
  307.6 52.0 %all-gather.29.cloned.1.call-start = ((), (), s32[]{:S(2)}) async-start(), calls=%async_computation.34 | async-start | bytes 2621440 | tf_op jit(solution)/shard_map/all_gather | solution.py:313
  355.4 52.0 %all-to-all-start.4 = ((bf16[8,2,128,512]{3,2,1,0:T(8,128)(2,1)}), bf16[8,2,128,512]{3,2,1,0:T(8,128)(2,1)S(1)}, u32[]{:S(2)}, u32[]{:S(2)}) async-start(bf16[8,2,128,512]{3,2,1,0:T(8,128)(2,1)} %bitcast.297), calls=%async_computation.4 | async-start | bytes 4194304 | tf_op jit(solution)/shard_map/all_to_all | solution.py:208
  359.1 26.1 %all-gather.31.cloned.1.call-start = ((), (), s32[]{:S(2)}) async-start(), calls=%async_computation.35 | async-start | bytes 2621440 | tf_op jit(solution)/shard_map/all_gather | solution.py:314
  407.5 17.2 %copy-start.49 = (bf16[8,2,128,512]{3,2,1,0:T(8,128)(2,1)}, bf16[8,2,128,512]{3,2,1,0:T(8,128)(2,1)S(1)}, u32[]{:S(2)}) copy-start(bf16[8,2,128,512]{3,2,1,0:T(8,128)(2,1)S(1)} %all-to-all-done.4) | copy-start | bytes 6291460
  407.5 17.2 %copy-start.104 = (bf16[1,1,512,2048]{3,2,1,0:T(8,128)(2,1)S(1)}, bf16[1,1,512,2048]{3,2,1,0:T(8,128)(2,1)}, u32[]{:S(2)}) copy-start(bf16[1,1,512,2048]{3,2,1,0:T(8,128)(2,1)} %all-gather.29.cloned.1.call-done) | copy-start | bytes 6291460
  430.7 52.1 %all-to-all-start.5 = ((bf16[8,2,128,512]{3,2,1,0:T(8,128)(2,1)}), bf16[8,2,128,512]{3,2,1,0:T(8,128)(2,1)S(1)}, u32[]{:S(2)}, u32[]{:S(2)}) async-start(bf16[8,2,128,512]{3,2,1,0:T(8,128)(2,1)} %bitcast.308), calls=%async_computation.5 | async-start | bytes 4194304 | tf_op jit(solution)/shard_map/all_to_all | solution.py:216
  484.1 52.4 %all-to-all-start.3 = ((bf16[8,2,128,512]{3,2,1,0:T(8,128)(2,1)}), bf16[8,2,128,512]{3,2,1,0:T(8,128)(2,1)}, u32[]{:S(2)}, u32[]{:S(2)}) async-start(bf16[8,2,128,512]{3,2,1,0:T(8,128)(2,1)} %bitcast.307), calls=%async_computation.3 | async-start | bytes 4194304 | tf_op jit(solution)/shard_map/all_to_all | solution.py:132
  562.7 8.8 slice-start.2
  587.8 7.1 copy-start.12
  587.8 7.1 copy-start.80
  587.8 7.1 copy-start.86
  587.8 7.1 copy-start.90
  587.8 7.1 copy-start.106
  618.4 52.1 %copy-start.103 = (bf16[1,1,2048,512]{3,2,1,0:T(8,128)(2,1)S(1)}, bf16[1,1,2048,512]{3,2,1,0:T(8,128)(2,1)}, u32[]{:S(2)}) copy-start(bf16[1,1,2048,512]{3,2,1,0:T(8,128)(2,1)} %all-gather.25.cloned.1.call-done) | copy-start | bytes 6291460
  670.5 17.5 %copy-start.50 = (bf16[8,2,128,512]{3,2,1,0:T(8,128)(2,1)}, bf16[8,2,128,512]{3,2,1,0:T(8,128)(2,1)S(1)}, u32[]{:S(2)}) copy-start(bf16[8,2,128,512]{3,2,1,0:T(8,128)(2,1)S(1)} %all_to_all.40) | copy-start | bytes 6291460
  670.5 17.5 %copy-start.102 = (bf16[1,1,512,2048]{3,2,1,0:T(8,128)(2,1)S(1)}, bf16[1,1,512,2048]{3,2,1,0:T(8,128)(2,1)}, u32[]{:S(2)}) copy-start(bf16[1,1,512,2048]{3,2,1,0:T(8,128)(2,1)} %all-gather.23.cloned.1.call-done) | copy-start | bytes 6291460
  694.1 51.9 %all-to-all-start.7 = ((bf16[8,2,128,512]{3,2,1,0:T(8,128)(2,1)}), bf16[8,2,128,512]{3,2,1,0:T(8,128)(2,1)}, u32[]{:S(2)}, u32[]{:S(2)}) async-start(bf16[8,2,128,512]{3,2,1,0:T(8,128)(2,1)} %bitcast.305), calls=%async_computation.7 | async-start | bytes 4194304 | tf_op jit(solution)/shard_map/all_to_all | solution.py:216
  698.7 156.1 %reduce-scatter.49.cloned.1.call-start = ((), (), s32[]{:S(2)}) async-start(), calls=%async_computation.39 | async-start | bytes 163840
  699.7 156.0 %reduce-scatter.45.cloned.1.call-start = ((), (), s32[]{:S(2)}) async-start(), calls=%async_computation.37 | async-start | bytes 163840
  700.6 155.9 %reduce-scatter.53.cloned.1.call-start = ((), (), s32[]{:S(2)}) async-start(), calls=%async_computation.41 | async-start | bytes 163840
  703.8 153.5 %reduce-scatter.51.cloned.1.call-start = ((), (), s32[]{:S(2)}) async-start(), calls=%async_computation.40 | async-start | bytes 163840
  706.4 155.1 %reduce-scatter.33.cloned.1.call-start = ((), (), s32[]{:S(2)}) async-start(), calls=%async_computation.25 | async-start | bytes 655360 | tf_op jit(solution)/shard_map/reduce_scatter | solution.py:272
  709.1 152.3 %reduce-scatter.29.cloned.1.call-start = ((), (), s32[]{:S(2)}) async-start(), calls=%async_computation.23 | async-start | bytes 1966080 | tf_op jit(solution)/shard_map/reduce_scatter | solution.py:272
  714.4 154.6 %reduce-scatter.31.cloned.1.call-start = ((), (), s32[]{:S(2)}) async-start(), calls=%async_computation.24 | async-start | bytes 655360 | tf_op jit(solution)/shard_map/reduce_scatter | solution.py:272
  765.5 10.8 slice-start
  780.8 118.7 %reduce-scatter.27.cloned.1.call-start = ((), (), s32[]{:S(2)}) async-start(), calls=%async_computation.22 | async-start | bytes 1966080 | tf_op jit(solution)/shard_map/reduce_scatter | solution.py:272
  795.3 6.9 copy-start.78
  795.3 6.9 copy-start.84
  795.3 6.9 copy-start.88
  795.3 6.9 copy-start.95
  807.6 113.8 %reduce-scatter.47.cloned.1.call-start = ((), (), s32[]{:S(2)}) async-start(), calls=%async_computation.38 | async-start | bytes 163840
  813.4 129.9 %reduce-scatter.43.cloned.1.call-start = ((), (), s32[]{:S(2)}) async-start(), calls=%async_computation.36 | async-start | bytes 163840
  814.3 163.2 %reduce-scatter.41.cloned.1.call-start = ((), (), s32[]{:S(2)}) async-start(), calls=%async_computation.29 | async-start | bytes 2621440 | tf_op jit(solution)/shard_map/reduce_scatter | solution.py:272
  824.4 186.7 %reduce-scatter.39.cloned.1.call-start = ((), (), s32[]{:S(2)}) async-start(), calls=%async_computation.28 | async-start | bytes 2621440 | tf_op jit(solution)/shard_map/reduce_scatter | solution.py:272
  834.6 210.8 %reduce-scatter.37.cloned.1.call-start = ((), (), s32[]{:S(2)}) async-start(), calls=%async_computation.27 | async-start | bytes 2621440 | tf_op jit(solution)/shard_map/reduce_scatter | solution.py:272
  844.8 234.2 %reduce-scatter.35.cloned.1.call-start = ((), (), s32[]{:S(2)}) async-start(), calls=%async_computation.26 | async-start | bytes 2621440 | tf_op jit(solution)/shard_map/reduce_scatter | solution.py:272
  854.8 306.4 %all-reduce.12.cloned.1.call-start = ((), (), s32[]{:S(2)}) async-start(), calls=%async_computation.42 | async-start | bytes 2097152 | tf_op jit(solution)/shard_map/psum | solution.py:278
  858.2 41.3 %copy-start.15 = (f32[788,512]{1,0:T(8,128)S(1)}, f32[788,512]{1,0:T(8,128)}, u32[]{:S(2)}) copy-start(f32[788,512]{1,0:T(8,128)} %copy-done.14) | copy-start | bytes 4841476
  (77 other events, 223.1 us)
Sparse Core Ops, SparseCore 0:
  10.2 22.3 all-gather.20
  34.7 22.5 all-gather.22
  116.8 23.9 all-gather.24
  193.3 22.2 all-gather.26
  310.3 23.8 all-gather.28
  361.1 23.9 all-gather.30
  702.0 20.9 reduce-scatter.48
  725.4 19.6 reduce-scatter.44
  747.5 19.6 reduce-scatter.52
  769.4 19.6 reduce-scatter.50
  792.2 21.6 reduce-scatter.32
  816.8 28.0 reduce-scatter.28
  847.4 21.6 reduce-scatter.30
  871.4 28.0 reduce-scatter.26
  901.8 19.6 reduce-scatter.46
  923.7 19.6 reduce-scatter.42
  946.3 31.1 reduce-scatter.40
  979.9 31.1 reduce-scatter.38
  1014.2 31.1 reduce-scatter.36
  1047.8 31.1 reduce-scatter.34
  1082.8 78.2 all-reduce.11
where the time goes:
time: 1180 us; the launch traced here: 1170 us
  waiting for transfers between devices  502 us (43%)
  local copies, waits for them, and re-layouts  218 us (18%)
  matrix products  206 us (17%)
  blocking collectives  123 us (10%)
  other arithmetic  72.7 us (6%)
  starting transfers between devices  33.4 us (3%)
  between operations  16.5 us (1%)
    reduce_scatter x8, waiting for transfers between devices, reduce_layer(): lax.psum_scatter(grad.astype(jnp.bfloat16), 'shard', scatter_dimension=di...  147 us
    psum x1, waiting for transfers between devices, reduce_layer(): lax.psum(part.astype(jnp.bfloat16), 'expert').astype(jnp.float32)  79.5 us
    all_to_all x2, waiting for transfers between devices, backward_layer(): lax.all_to_all(d_rows, 'expert', split_axis=0, concat_axis=0, tiled=True)  70.1 us
    all_to_all x2, waiting for transfers between devices, forward_layer(): lax.all_to_all(sending, 'expert', split_axis=0, concat_axis=0, tiled=True)  70 us
    all_to_all x2, waiting for transfers between devices, forward_layer(): lax.all_to_all(expert_rows.reshape(experts, blocks, capacity, D), 'expert...  60.4 us
    dot_general x10, matrix products, dot_last(): lax.dot_general(left, right, (((1,), (1,)), ((), ())), preferred_element_...  58.6 us
    dot_general x10, matrix products, dot_first(): lax.dot_general(left, right, (((0,), (0,)), ((), ())), preferred_element_...  57.7 us
    all_to_all x1, blocking collectives, backward_layer(): lax.all_to_all(d_slots, 'expert', split_axis=0, concat_axis=0, tiled=True)  52.1 us
  transfers between devices with their start and end apart: 28, of which 17 were waited for; matrix products, arithmetic and copies ran while one was open for 25% of the time, Pallas kernels for 0%

commit v1 on v0

--- a/solution.py
+++ b/solution.py
@@ -274,8 +274,10 @@
         ).astype(jnp.float32)
         for grad, dim in zip(layer_grads, SCATTER_DIMS)
     ]
+    open_matrix = lambda m, mesh_ax: jnp.sum(lax.all_gather(m, mesh_ax), 0)
     replicated = [
-        lax.psum(part.astype(jnp.bfloat16), "expert").astype(jnp.float32) for part in scattered[:5]
+        open_matrix(part.astype(jnp.bfloat16), "expert").astype(jnp.float32)
+        for part in scattered[:5]
     ]
     return replicated + scattered[5:]
 

time: 1180 us -> 1330 us (1.13)
  blocking collectives: 123 us -> 232 us
  waiting for transfers between devices: 502 us -> 538 us
    all_gather x0 -> x4, waiting for transfers between devices: none -> 157 us  [reduce_layer(): open_matrix = lambda m, mesh_ax: jnp.sum(lax.all_gather(m, mesh_ax), 0)]
    all_gather x0 -> x6, blocking collectives: none -> 131 us  [reduce_layer(): open_matrix = lambda m, mesh_ax: jnp.sum(lax.all_gather(m, mesh_ax), 0)]
    psum x1 -> x0, waiting for transfers between devices: 79.5 us -> none  [reduce_layer(): lax.psum(part.astype(jnp.bfloat16), 'expert').astype(jnp.float32)]
    reduce_scatter x8, waiting for transfers between devices: 147 us -> 111 us  [reduce_layer(): lax.psum_scatter(grad.astype(jnp.bfloat16), 'shard', scatter_dimension=di...]
    psum x1 -> x0, blocking collectives: 21.6 us -> none  [reduce_layer(): lax.psum(part.astype(jnp.bfloat16), 'expert').astype(jnp.float32)]
    unnamed x27 -> x30, waiting for transfers between devices: 42.1 us -> 32 us
    unnamed x251 -> x255, local copies, waits for them, and re-layouts: 49 us -> 48.8 us
  transfers between devices with their start and end apart: 28 -> 31, of which waited for: 17 -> 19; matrix products, arithmetic and copies ran while one was open for 25% -> 23% of each run, Pallas kernels for 0% -> 0%
where the time goes in v1:
time: 1330 us; the launch traced here: 1320 us
  waiting for transfers between devices  538 us (40%)
  blocking collectives  232 us (17%)
  local copies, waits for them, and re-layouts  218 us (16%)
  matrix products  206 us (15%)
  other arithmetic  74.3 us (6%)
  starting transfers between devices  33.4 us (3%)
  between operations  16.6 us (1%)
    all_gather x4, waiting for transfers between devices, reduce_layer(): open_matrix = lambda m, mesh_ax: jnp.sum(lax.all_gather(m, mesh_ax), 0)  157 us
    all_gather x6, blocking collectives, reduce_layer(): open_matrix = lambda m, mesh_ax: jnp.sum(lax.all_gather(m, mesh_ax), 0)  131 us
    reduce_scatter x8, waiting for transfers between devices, reduce_layer(): lax.psum_scatter(grad.astype(jnp.bfloat16), 'shard', scatter_dimension=di...  111 us
    all_to_all x2, waiting for transfers between devices, backward_layer(): lax.all_to_all(d_rows, 'expert', split_axis=0, concat_axis=0, tiled=True)  74.3 us
    all_to_all x2, waiting for transfers between devices, forward_layer(): lax.all_to_all(sending, 'expert', split_axis=0, concat_axis=0, tiled=True)  70 us
    all_to_all x2, waiting for transfers between devices, forward_layer(): lax.all_to_all(expert_rows.reshape(experts, blocks, capacity, D), 'expert...  61 us
    dot_general x10, matrix products, dot_last(): lax.dot_general(left, right, (((1,), (1,)), ((), ())), preferred_element_...  58.8 us
    dot_general x10, matrix products, dot_first(): lax.dot_general(left, right, (((0,), (0,)), ((), ())), preferred_element_...  57.5 us
  transfers between devices with their start and end apart: 31, of which 19 were waited for; matrix products, arithmetic and copies ran while one was open for 23% of the time, Pallas kernels for 0%

profile of v1, /device:TPU:0, one launch (start us, length us, event | category | flops | bytes accessed | tf_op | source)
XLA Modules:
  0.0 1318.8 jit_solution(10368019118343551874)
XLA Ops:
  10.7 6.0 all-gather.1
  16.7 5.4 all-gather
  24.2 16.5 %fusion.16 = s32[2,788]{0,1:T(8,128)S(1)} fusion(s32[2,788]{0,1:T(8,128)S(1)} %copy.267, s32[2,788]{1,0:T(2,128)S(1)} %get-tuple-element.95, s32[2,788]{1,0:T(2,128)S(1)} %get-tuple-element.94, s32[2,788]{0,1:T(8,128)S(1)} %copy.266), kind=kLoop, calls=%fused_computation.42 | loop fusion | flops 6207864 | bytes 31520 | tf_op jit(solution)/shard_map/vmap()/reduce_sum | solution.py:47
  43.9 8.8 scatter_custom_fusion
  52.9 8.3 all-gather.3
  65.6 7.2 reshape.825
  98.7 9.2 gather_fusion
  107.9 6.1 all-to-all-start
  115.3 47.5 %all-to-all-done = bf16[8,2,128,512]{3,2,1,0:T(8,128)(2,1)} async-done(((bf16[8,2,128,512]{3,2,1,0:T(8,128)(2,1)}), bf16[8,2,128,512]{3,2,1,0:T(8,128)(2,1)}, u32[]{:S(2)}, u32[]{:S(2)}) %all-to-all-start) | async-done | bytes 2097184 | tf_op jit(solution)/shard_map/all_to_all | solution.py:125
  162.8 14.1 %multiply_convert_fusion.1 = (bf16[2048,2048]{1,0:T(8,128)(2,1)}, f32[2048,2048]{1,0:T(8,128)}) fusion(bf16[2048,512]{1,0:T(8,128)(2,1)} %bitcast.20, bf16[1,1,512,2048]{3,2,1,0:T(8,128)(2,1)} %all-gather.41.cloned.1.call-done), kind=kOutput, calls=%fused_computation.28 | convolution fusion | flops 4332716032 | bytes 29360128 | tf_op jit(solution)/shard_map/dot_general | solution.py:127
  176.9 9.8 convolution_convert_fusion.11
  192.4 5.1 all-gather.8
  197.5 5.0 all-gather.7
  202.5 5.3 all-gather.4
  207.9 9.0 all-gather.10
  218.0 21.0 %all-to-all-done.1 = bf16[8,2,128,512]{3,2,1,0:T(8,128)(2,1)} async-done(((bf16[8,2,128,512]{3,2,1,0:T(8,128)(2,1)}), bf16[8,2,128,512]{3,2,1,0:T(8,128)(2,1)}, u32[]{:S(2)}, u32[]{:S(2)}) %all-to-all-start.1) | async-done | bytes 2097184 | tf_op jit(solution)/shard_map/all_to_all | solution.py:132
  240.8 6.4 gather_fusion.1
  261.6 7.2 reshape.826
  294.0 9.2 gather_fusion.2
  315.2 5.2 all-gather.11
  323.7 9.2 gather_fusion.4
  332.9 22.5 %all-to-all-done.2 = bf16[8,2,128,512]{3,2,1,0:T(8,128)(2,1)} async-done(((bf16[8,2,128,512]{3,2,1,0:T(8,128)(2,1)}), bf16[8,2,128,512]{3,2,1,0:T(8,128)(2,1)}, u32[]{:S(2)}, u32[]{:S(2)}) %all-to-all-start.2) | async-done | bytes 2097184 | tf_op jit(solution)/shard_map/all_to_all | solution.py:125
  359.6 14.4 %multiply_convert_fusion = (bf16[2048,2048]{1,0:T(8,128)(2,1)}, f32[2048,2048]{1,0:T(8,128)}) fusion(bf16[2048,512]{1,0:T(8,128)(2,1)} %bitcast.38, bf16[1,1,512,2048]{3,2,1,0:T(8,128)(2,1)} %all-gather.47.cloned.1.call-done), kind=kOutput, calls=%fused_computation.27 | convolution fusion | flops 4332716032 | bytes 29360128 | tf_op jit(solution)/shard_map/dot_general | solution.py:127
  374.0 11.0 all-gather.49.cloned.1.call-done
  385.1 22.3 %all-to-all-done.4 = bf16[8,2,128,512]{3,2,1,0:T(8,128)(2,1)S(1)} async-done(((bf16[8,2,128,512]{3,2,1,0:T(8,128)(2,1)}), bf16[8,2,128,512]{3,2,1,0:T(8,128)(2,1)S(1)}, u32[]{:S(2)}, u32[]{:S(2)}) %all-to-all-start.4) | async-done | bytes 2097184 | tf_op jit(solution)/shard_map/all_to_all | solution.py:208
  407.4 17.1 %fusion.13 = bf16[2048,2048]{1,0:T(8,128)(2,1)S(1)} fusion(f32[2048,2048]{1,0:T(8,128)} %get-tuple-element.85, bf16[2048,512]{1,0:T(8,128)(2,1)S(1)} %bitcast.315, bf16[1,1,2048,512]{3,2,1,0:T(8,128)(2,1)} %all-gather.49.cloned.1.call-done), kind=kOutput, calls=%fused_computation.26 | convolution fusion | flops 4378853376 | bytes 29360128 | tf_op jit(solution)/shard_map/dot_general | solution.py:36
  424.6 6.1 convolution_convert_fusion.9
  434.3 9.8 convolution_convert_fusion.10
  444.1 38.6 %all-to-all-done.5 = bf16[8,2,128,512]{3,2,1,0:T(8,128)(2,1)S(1)} async-done(((bf16[8,2,128,512]{3,2,1,0:T(8,128)(2,1)}), bf16[8,2,128,512]{3,2,1,0:T(8,128)(2,1)S(1)}, u32[]{:S(2)}, u32[]{:S(2)}) %all-to-all-start.5) | async-done | bytes 2097184 | tf_op jit(solution)/shard_map/all_to_all | solution.py:216
  490.5 6.0 gather_fusion.5
  496.5 39.9 %all-to-all-done.3 = bf16[8,2,128,512]{3,2,1,0:T(8,128)(2,1)} async-done(((bf16[8,2,128,512]{3,2,1,0:T(8,128)(2,1)}), bf16[8,2,128,512]{3,2,1,0:T(8,128)(2,1)}, u32[]{:S(2)}, u32[]{:S(2)}) %all-to-all-start.3) | async-done | bytes 2097184 | tf_op jit(solution)/shard_map/all_to_all | solution.py:132
  538.2 6.0 gather_fusion.3
  587.9 7.0 convert_element_type.400
  609.3 9.2 gather_fusion.6
  618.5 52.1 %all_to_all.40 = bf16[8,2,128,512]{3,2,1,0:T(8,128)(2,1)S(1)} all-to-all(bf16[8,2,128,512]{3,2,1,0:T(8,128)(2,1)} %bitcast.311), channel_id=1, replica_groups=mesh['expert'=8,'shard'=4] {'expert'}, dimensions={0} | all-to-all | bytes 4194304 | tf_op jit(solution)/shard_map/all_to_all | solution.py:208
  670.6 17.5 %fusion.6 = bf16[2048,2048]{1,0:T(8,128)(2,1)S(1)} fusion(f32[2048,2048]{1,0:T(8,128)} %get-tuple-element.75, bf16[2048,512]{1,0:T(8,128)(2,1)S(1)} %bitcast.317, bf16[1,1,2048,512]{3,2,1,0:T(8,128)(2,1)S(1)} %copy-done.106), kind=kOutput, calls=%fused_computation.19 | convolution fusion | flops 4378853376 | bytes 29360128 | tf_op jit(solution)/shard_map/dot_general | solution.py:36
  688.1 6.1 convolution_convert_fusion.8
  704.5 5.6 convolution_convert_fusion.6
  710.3 35.7 %all-to-all-done.7 = bf16[8,2,128,512]{3,2,1,0:T(8,128)(2,1)} async-done(((bf16[8,2,128,512]{3,2,1,0:T(8,128)(2,1)}), bf16[8,2,128,512]{3,2,1,0:T(8,128)(2,1)}, u32[]{:S(2)}, u32[]{:S(2)}) %all-to-all-start.7) | async-done | bytes 2097184 | tf_op jit(solution)/shard_map/all_to_all | solution.py:216
  747.7 6.0 gather_fusion.7
  770.9 5.3 fusion.57
  781.1 6.4 multiply_convert_fusion.2
  795.2 6.9 convert_element_type.411
  802.2 5.2 convolution_convert_fusion.7
  812.3 4.7 multiply_reduce_fusion.11
  818.8 9.9 fusion.32
  828.7 9.9 fusion.31
  839.0 9.9 fusion.30
  849.0 10.0 fusion.29
  861.9 18.6 %all-gather.27 = bf16[8,2,128]{2,1,0:T(2,128)(2,1)S(1)} all-gather(bf16[1,2,128]{2,1,0:T(2,128)(2,1)S(1)} %bitcast.360), channel_id=19, replica_groups=mesh['expert'=8,'shard'=4] {'expert'}, dimensions={0}, use_global_device_ids=true | all-gather | bytes 4608 | tf_op jit(solution)/shard_map/all_gather | solution.py:277
  881.3 18.7 %all-gather.25 = bf16[8,2,128]{2,1,0:T(2,128)(2,1)S(1)} all-gather(bf16[1,2,128]{2,1,0:T(2,128)(2,1)S(1)} %bitcast.361), channel_id=17, replica_groups=mesh['expert'=8,'shard'=4] {'expert'}, dimensions={0}, use_global_device_ids=true | all-gather | bytes 4608 | tf_op jit(solution)/shard_map/all_gather | solution.py:277
  901.6 21.1 %reduce-scatter.51.cloned.1.call-done = bf16[128,8]{1,0:T(8,128)(2,1)} async-done(((bf16[512,8]{1,0:T(8,128)(2,1)}), bf16[128,8]{1,0:T(8,128)(2,1)}) %reduce-scatter.51.cloned.1.call-update) | async-done | bytes 2064
  923.6 26.2 %all-gather.23 = bf16[1024,8]{0,1:T(8,128)(2,1)S(1)} all-gather(bf16[128,8]{0,1:T(8,128)(2,1)S(1)} %copy.320), channel_id=25, replica_groups=mesh['expert'=8,'shard'=4] {'expert'}, dimensions={0}, use_global_device_ids=true | all-gather | bytes 18432 | tf_op jit(solution)/shard_map/all_gather | solution.py:277
  949.8 26.3 %all-gather.22 = bf16[1024,8]{0,1:T(8,128)(2,1)S(1)} all-gather(bf16[128,8]{0,1:T(8,128)(2,1)S(1)} %copy.318), channel_id=24, replica_groups=mesh['expert'=8,'shard'=4] {'expert'}, dimensions={0}, use_global_device_ids=true | all-gather | bytes 18432 | tf_op jit(solution)/shard_map/all_gather | solution.py:277
  980.9 4.8 reduce-scatter.47.cloned.1.call-done
  986.5 20.5 %all-gather.26 = bf16[8,2,128]{2,1,0:T(2,128)(2,1)S(1)} all-gather(bf16[1,2,128]{2,1,0:T(2,128)(2,1)S(1)} %bitcast.362), channel_id=18, replica_groups=mesh['expert'=8,'shard'=4] {'expert'}, dimensions={0}, use_global_device_ids=true | all-gather | bytes 4608 | tf_op jit(solution)/shard_map/all_gather | solution.py:277
  1009.0 20.5 %all-gather.24 = bf16[8,2,128]{2,1,0:T(2,128)(2,1)S(1)} all-gather(bf16[1,2,128]{2,1,0:T(2,128)(2,1)S(1)} %bitcast.363), channel_id=16, replica_groups=mesh['expert'=8,'shard'=4] {'expert'}, dimensions={0}, use_global_device_ids=true | all-gather | bytes 4608 | tf_op jit(solution)/shard_map/all_gather | solution.py:277
  1030.7 11.6 reduce-scatter.41.cloned.1.call-done
  1042.4 33.7 %reduce-scatter.39.cloned.1.call-done = bf16[1,512,512]{2,1,0:T(8,128)(2,1)} async-done(((bf16[1,2048,512]{2,1,0:T(8,128)(2,1)}), bf16[1,512,512]{2,1,0:T(8,128)(2,1)}) %reduce-scatter.39.cloned.1.call-update) | async-done | bytes 524304 | tf_op jit(solution)/shard_map/reduce_scatter | solution.py:272
  1078.7 31.5 %reduce-scatter.37.cloned.1.call-done = bf16[1,128,2048]{2,1,0:T(8,128)(2,1)} async-done(((bf16[1,512,2048]{2,1,0:T(8,128)(2,1)}), bf16[1,128,2048]{2,1,0:T(8,128)(2,1)}) %reduce-scatter.37.cloned.1.call-update) | async-done | bytes 524304 | tf_op jit(solution)/shard_map/reduce_scatter | solution.py:272
  1110.2 33.7 %reduce-scatter.35.cloned.1.call-done = bf16[1,128,2048]{2,1,0:T(8,128)(2,1)} async-done(((bf16[1,512,2048]{2,1,0:T(8,128)(2,1)}), bf16[1,128,2048]{2,1,0:T(8,128)(2,1)}) %reduce-scatter.35.cloned.1.call-update) | async-done | bytes 524304 | tf_op jit(solution)/shard_map/reduce_scatter | solution.py:272
  1146.6 59.6 %all-gather.53.cloned.1.call-done = bf16[1024,1536]{1,0:T(8,128)(2,1)} async-done(((bf16[128,1536]{1,0:T(8,128)(2,1)}), bf16[1024,1536]{1,0:T(8,128)(2,1)}) %all-gather.53.cloned.1.call-update) | async-done | bytes 3145744 | tf_op jit(solution)/shard_map/all_gather | solution.py:277
  1208.6 38.7 %all-gather.55.cloned.1.call-done = bf16[1024,512]{1,0:T(8,128)(2,1)} async-done(((bf16[128,512]{1,0:T(8,128)(2,1)}), bf16[1024,512]{1,0:T(8,128)(2,1)}) %all-gather.55.cloned.1.call-update) | async-done | bytes 1048592 | tf_op jit(solution)/shard_map/all_gather | solution.py:277
  1249.5 58.6 %all-gather.51.cloned.1.call-done = bf16[1024,1536]{1,0:T(8,128)(2,1)} async-done(((bf16[128,1536]{1,0:T(8,128)(2,1)}), bf16[1024,1536]{1,0:T(8,128)(2,1)}) %all-gather.51.cloned.1.call-update) | async-done | bytes 3145744 | tf_op jit(solution)/shard_map/all_gather | solution.py:277
  (529 shorter events, 255.2 us)
Async XLA Ops:
  7.2 14.9 %copy-start.95 = (s32[788]{0:T(1024)S(1)}, s32[788]{0:T(1024)}, u32[]{:S(2)}) copy-start(s32[788]{0:T(1024)} %param.13) | copy-start | bytes 9460
  7.2 15.0 %copy-start.9 = (f32[788,512]{1,0:T(8,128)S(1)}, f32[788,512]{1,0:T(8,128)}, u32[]{:S(2)}) copy-start(f32[788,512]{1,0:T(8,128)} %param.11) | copy-start | bytes 4841476
  7.2 54.0 %all-gather.39.cloned.1.call-start = ((), (), s32[]{:S(2)}) async-start(), calls=%async_computation.30 | async-start | bytes 1966080 | tf_op jit(solution)/shard_map/all_gather | solution.py:312
  9.5 105.8 %all-gather.41.cloned.1.call-start = ((), (), s32[]{:S(2)}) async-start(), calls=%async_computation.31 | async-start | bytes 2621440 | tf_op jit(solution)/shard_map/all_gather | solution.py:315
  10.6 12.3 copy-start.92
  10.6 12.4 copy-start.57
  22.1 39.1 %copy-start.88 = (f32[1,1,512]{2,1,0:T(1,128)}, f32[1,1,512]{2,1,0:T(1,128)S(1)}, u32[]{:S(2)}) copy-start(f32[1,1,512]{2,1,0:T(1,128)S(1)} %get-tuple-element.63) | copy-start | bytes 6148
  22.1 75.8 %copy-start.82 = (f32[1,1,512]{2,1,0:T(1,128)}, f32[1,1,512]{2,1,0:T(1,128)S(1)}, u32[]{:S(2)}) copy-start(f32[1,1,512]{2,1,0:T(1,128)S(1)} %get-tuple-element.62) | copy-start | bytes 6148
  22.1 39.1 %copy-start.97 = (f32[1,1,512]{2,1,0:T(1,128)}, f32[1,1,512]{2,1,0:T(1,128)S(1)}, u32[]{:S(2)}) copy-start(f32[1,1,512]{2,1,0:T(1,128)S(1)} %get-tuple-element.65) | copy-start | bytes 6148
  22.4 38.8 %copy-start.78 = (f32[788]{0:T(1024)}, f32[788]{0:T(1024)S(1)}, u32[]{:S(2)}) copy-start(f32[788]{0:T(1024)S(1)} %broadcast_multiply_fusion.3) | copy-start | bytes 9460
  22.8 38.4 %copy-start.84 = (f32[788]{0:T(1024)}, f32[788]{0:T(1024)S(1)}, u32[]{:S(2)}) copy-start(f32[788]{0:T(1024)S(1)} %fusion.115) | copy-start | bytes 9460
  23.7 19.3 %copy-start.104 = (s32[2]{0:T(128)S(1)}, s32[2]{0:T(128)}, u32[]{:S(2)}) copy-start(s32[2]{0:T(128)} %constant.154) | copy-start | bytes 28
  23.7 19.4 %copy-start.103 = (s32[2]{0:T(128)S(1)}, s32[2]{0:T(128)}, u32[]{:S(2)}) copy-start(s32[2]{0:T(128)} %constant.151) | copy-start | bytes 28
  98.2 118.6 %copy-start.22 = (bf16[788,512]{1,0:T(8,128)(2,1)}, bf16[788,512]{1,0:T(8,128)(2,1)S(1)}, u32[]{:S(2)}) copy-start(bf16[788,512]{1,0:T(8,128)(2,1)S(1)} %add_convert_fusion.2) | copy-start | bytes 2420740
  107.9 54.9 %all-to-all-start = ((bf16[8,2,128,512]{3,2,1,0:T(8,128)(2,1)}), bf16[8,2,128,512]{3,2,1,0:T(8,128)(2,1)}, u32[]{:S(2)}, u32[]{:S(2)}) async-start(bf16[8,2,128,512]{3,2,1,0:T(8,128)(2,1)} %bitcast.310), calls=%async_computation | async-start | bytes 4194304 | tf_op jit(solution)/shard_map/all_to_all | solution.py:125
  113.9 62.9 %all-gather.43.cloned.1.call-start = ((), (), s32[]{:S(2)}) async-start(), calls=%async_computation.32 | async-start | bytes 2621440 | tf_op jit(solution)/shard_map/all_gather | solution.py:316
  186.7 15.8 %copy-start.96 = (bf16[2,128,8]{1,2,0:T(8,128)(2,1)S(1)}, bf16[2,128,8]{1,2,0:T(8,128)(2,1)}, u32[]{:S(2)}) copy-start(bf16[2,128,8]{1,2,0:T(8,128)(2,1)} %param.18) | copy-start | bytes 12292
  186.7 52.4 %all-to-all-start.1 = ((bf16[8,2,128,512]{3,2,1,0:T(8,128)(2,1)}), bf16[8,2,128,512]{3,2,1,0:T(8,128)(2,1)}, u32[]{:S(2)}, u32[]{:S(2)}) async-start(bf16[8,2,128,512]{3,2,1,0:T(8,128)(2,1)} %bitcast.319), calls=%async_computation.1 | async-start | bytes 4194304 | tf_op jit(solution)/shard_map/all_to_all | solution.py:132
  191.2 66.0 %all-gather.45.cloned.1.call-start = ((), (), s32[]{:S(2)}) async-start(), calls=%async_computation.33 | async-start | bytes 1966080 | tf_op jit(solution)/shard_map/all_gather | solution.py:312
  207.9 32.9 %copy-start.66 = (bf16[1,512,8]{1,2,0:T(8,128)(2,1)}, bf16[1,512,8]{1,2,0:T(8,128)(2,1)S(1)}, u32[]{:S(2)}) copy-start(bf16[1,512,8]{1,2,0:T(8,128)(2,1)S(1)} %all-gather.4) | copy-start | bytes 24580
  216.9 40.3 %copy-start.90 = (f32[1,1,512]{2,1,0:T(1,128)}, f32[1,1,512]{2,1,0:T(1,128)S(1)}, u32[]{:S(2)}) copy-start(f32[1,1,512]{2,1,0:T(1,128)S(1)} %get-tuple-element.59) | copy-start | bytes 6148
  216.9 40.3 %copy-start.99 = (f32[1,1,512]{2,1,0:T(1,128)}, f32[1,1,512]{2,1,0:T(1,128)S(1)}, u32[]{:S(2)}) copy-start(f32[1,1,512]{2,1,0:T(1,128)S(1)} %get-tuple-element.61) | copy-start | bytes 6148
  217.2 23.6 %copy-start.62 = (f32[788]{0:T(1024)}, f32[788]{0:T(1024)S(1)}, u32[]{:S(2)}) copy-start(f32[788]{0:T(1024)S(1)} %get-tuple-element.76) | copy-start | bytes 9460
  217.9 23.0 %copy-start.68 = (f32[788]{0:T(1024)}, f32[788]{0:T(1024)S(1)}, u32[]{:S(2)}) copy-start(f32[788]{0:T(1024)S(1)} %fusion.104) | copy-start | bytes 9460
  256.7 34.4 %copy-start.11 = (f32[788,512]{1,0:T(8,128)}, f32[788,512]{1,0:T(8,128)S(1)}, u32[]{:S(2)}) copy-start(f32[788,512]{1,0:T(8,128)S(1)} %get-tuple-element.32) | copy-start | bytes 4841476
  293.6 26.8 %copy-start.24 = (bf16[788,512]{1,0:T(8,128)(2,1)}, bf16[788,512]{1,0:T(8,128)(2,1)S(1)}, u32[]{:S(2)}) copy-start(bf16[788,512]{1,0:T(8,128)(2,1)S(1)} %add_convert_fusion) | copy-start | bytes 2420740
  303.2 52.2 %all-to-all-start.2 = ((bf16[8,2,128,512]{3,2,1,0:T(8,128)(2,1)}), bf16[8,2,128,512]{3,2,1,0:T(8,128)(2,1)}, u32[]{:S(2)}, u32[]{:S(2)}) async-start(bf16[8,2,128,512]{3,2,1,0:T(8,128)(2,1)} %bitcast.308), calls=%async_computation.2 | async-start | bytes 4194304 | tf_op jit(solution)/shard_map/all_to_all | solution.py:125
  307.6 52.0 %all-gather.47.cloned.1.call-start = ((), (), s32[]{:S(2)}) async-start(), calls=%async_computation.34 | async-start | bytes 2621440 | tf_op jit(solution)/shard_map/all_gather | solution.py:315
  355.4 52.0 %all-to-all-start.4 = ((bf16[8,2,128,512]{3,2,1,0:T(8,128)(2,1)}), bf16[8,2,128,512]{3,2,1,0:T(8,128)(2,1)S(1)}, u32[]{:S(2)}, u32[]{:S(2)}) async-start(bf16[8,2,128,512]{3,2,1,0:T(8,128)(2,1)} %bitcast.309), calls=%async_computation.4 | async-start | bytes 4194304 | tf_op jit(solution)/shard_map/all_to_all | solution.py:208
  359.0 26.1 %all-gather.49.cloned.1.call-start = ((), (), s32[]{:S(2)}) async-start(), calls=%async_computation.35 | async-start | bytes 2621440 | tf_op jit(solution)/shard_map/all_gather | solution.py:316
  407.4 17.2 %copy-start.48 = (bf16[8,2,128,512]{3,2,1,0:T(8,128)(2,1)}, bf16[8,2,128,512]{3,2,1,0:T(8,128)(2,1)S(1)}, u32[]{:S(2)}) copy-start(bf16[8,2,128,512]{3,2,1,0:T(8,128)(2,1)S(1)} %all-to-all-done.4) | copy-start | bytes 6291460
  407.4 17.2 %copy-start.107 = (bf16[1,1,512,2048]{3,2,1,0:T(8,128)(2,1)S(1)}, bf16[1,1,512,2048]{3,2,1,0:T(8,128)(2,1)}, u32[]{:S(2)}) copy-start(bf16[1,1,512,2048]{3,2,1,0:T(8,128)(2,1)} %all-gather.47.cloned.1.call-done) | copy-start | bytes 6291460
  430.7 52.1 %all-to-all-start.5 = ((bf16[8,2,128,512]{3,2,1,0:T(8,128)(2,1)}), bf16[8,2,128,512]{3,2,1,0:T(8,128)(2,1)S(1)}, u32[]{:S(2)}, u32[]{:S(2)}) async-start(bf16[8,2,128,512]{3,2,1,0:T(8,128)(2,1)} %bitcast.321), calls=%async_computation.5 | async-start | bytes 4194304 | tf_op jit(solution)/shard_map/all_to_all | solution.py:216
  484.0 52.4 %all-to-all-start.3 = ((bf16[8,2,128,512]{3,2,1,0:T(8,128)(2,1)}), bf16[8,2,128,512]{3,2,1,0:T(8,128)(2,1)}, u32[]{:S(2)}, u32[]{:S(2)}) async-start(bf16[8,2,128,512]{3,2,1,0:T(8,128)(2,1)} %bitcast.320), calls=%async_computation.3 | async-start | bytes 4194304 | tf_op jit(solution)/shard_map/all_to_all | solution.py:132
  562.8 8.8 slice-start.2
  587.9 7.1 copy-start.12
  587.9 7.1 copy-start.81
  587.9 7.1 copy-start.87
  587.9 7.1 copy-start.91
  587.9 7.1 copy-start.108
  618.5 52.1 %copy-start.106 = (bf16[1,1,2048,512]{3,2,1,0:T(8,128)(2,1)S(1)}, bf16[1,1,2048,512]{3,2,1,0:T(8,128)(2,1)}, u32[]{:S(2)}) copy-start(bf16[1,1,2048,512]{3,2,1,0:T(8,128)(2,1)} %all-gather.43.cloned.1.call-done) | copy-start | bytes 6291460
  670.6 17.5 %copy-start.49 = (bf16[8,2,128,512]{3,2,1,0:T(8,128)(2,1)}, bf16[8,2,128,512]{3,2,1,0:T(8,128)(2,1)S(1)}, u32[]{:S(2)}) copy-start(bf16[8,2,128,512]{3,2,1,0:T(8,128)(2,1)S(1)} %all_to_all.40) | copy-start | bytes 6291460
  670.6 17.5 %copy-start.105 = (bf16[1,1,512,2048]{3,2,1,0:T(8,128)(2,1)S(1)}, bf16[1,1,512,2048]{3,2,1,0:T(8,128)(2,1)}, u32[]{:S(2)}) copy-start(bf16[1,1,512,2048]{3,2,1,0:T(8,128)(2,1)} %all-gather.41.cloned.1.call-done) | copy-start | bytes 6291460
  694.2 51.8 %all-to-all-start.7 = ((bf16[8,2,128,512]{3,2,1,0:T(8,128)(2,1)}), bf16[8,2,128,512]{3,2,1,0:T(8,128)(2,1)}, u32[]{:S(2)}, u32[]{:S(2)}) async-start(bf16[8,2,128,512]{3,2,1,0:T(8,128)(2,1)} %bitcast.61), calls=%async_computation.7 | async-start | bytes 4194304 | tf_op jit(solution)/shard_map/all_to_all | solution.py:216
  698.7 112.9 %reduce-scatter.33.cloned.1.call-start = ((), (), s32[]{:S(2)}) async-start(), calls=%async_computation.25 | async-start | bytes 655360 | tf_op jit(solution)/shard_map/reduce_scatter | solution.py:272
  702.2 156.9 %reduce-scatter.29.cloned.1.call-start = ((), (), s32[]{:S(2)}) async-start(), calls=%async_computation.23 | async-start | bytes 1966080 | tf_op jit(solution)/shard_map/reduce_scatter | solution.py:272
  710.1 149.7 %reduce-scatter.31.cloned.1.call-start = ((), (), s32[]{:S(2)}) async-start(), calls=%async_computation.24 | async-start | bytes 655360 | tf_op jit(solution)/shard_map/reduce_scatter | solution.py:272
  765.5 10.7 slice-start
  780.7 79.9 %reduce-scatter.27.cloned.1.call-start = ((), (), s32[]{:S(2)}) async-start(), calls=%async_computation.22 | async-start | bytes 1966080 | tf_op jit(solution)/shard_map/reduce_scatter | solution.py:272
  807.4 53.7 %reduce-scatter.49.cloned.1.call-start = ((), (), s32[]{:S(2)}) async-start(), calls=%async_computation.43 | async-start | bytes 163840
  808.3 72.2 %reduce-scatter.45.cloned.1.call-start = ((), (), s32[]{:S(2)}) async-start(), calls=%async_computation.41 | async-start | bytes 163840
  809.2 91.6 %reduce-scatter.53.cloned.1.call-start = ((), (), s32[]{:S(2)}) async-start(), calls=%async_computation.45 | async-start | bytes 163840
  810.4 112.4 %reduce-scatter.51.cloned.1.call-start = ((), (), s32[]{:S(2)}) async-start(), calls=%async_computation.44 | async-start | bytes 163840
  811.5 165.3 %all-gather.57.cloned.1.call-start = ((), (), s32[]{:S(2)}) async-start(), calls=%async_computation.39 | async-start | bytes 1179648 | tf_op jit(solution)/shard_map/all_gather | solution.py:277
  812.1 173.6 %reduce-scatter.47.cloned.1.call-start = ((), (), s32[]{:S(2)}) async-start(), calls=%async_computation.42 | async-start | bytes 163840
  817.8 190.4 %reduce-scatter.43.cloned.1.call-start = ((), (), s32[]{:S(2)}) async-start(), calls=%async_computation.40 | async-start | bytes 163840
  818.7 223.6 %reduce-scatter.41.cloned.1.call-start = ((), (), s32[]{:S(2)}) async-start(), calls=%async_computation.29 | async-start | bytes 2621440 | tf_op jit(solution)/shard_map/reduce_scatter | solution.py:272
  828.7 247.4 %reduce-scatter.39.cloned.1.call-start = ((), (), s32[]{:S(2)}) async-start(), calls=%async_computation.28 | async-start | bytes 2621440 | tf_op jit(solution)/shard_map/reduce_scatter | solution.py:272
  838.7 271.5 %reduce-scatter.37.cloned.1.call-start = ((), (), s32[]{:S(2)}) async-start(), calls=%async_computation.27 | async-start | bytes 2621440 | tf_op jit(solution)/shard_map/reduce_scatter | solution.py:272
  848.9 295.0 %reduce-scatter.35.cloned.1.call-start = ((), (), s32[]{:S(2)}) async-start(), calls=%async_computation.26 | async-start | bytes 2621440 | tf_op jit(solution)/shard_map/reduce_scatter | solution.py:272
  859.0 119.2 %copy-start.73 = (f32[788]{0:T(1024)S(1)}, f32[788]{0:T(1024)}, u32[]{:S(2)}) copy-start(f32[788]{0:T(1024)} %copy-done.72) | copy-start | bytes 9460
  859.0 347.2 %all-gather.53.cloned.1.call-start = ((), (), s32[]{:S(2)}) async-start(), calls=%async_computation.37 | async-start | bytes 3538944 | tf_op jit(solution)/shard_map/all_gather | solution.py:277
  859.7 387.5 %all-gather.55.cloned.1.call-start = ((), (), s32[]{:S(2)}) async-start(), calls=%async_computation.38 | async-start | bytes 1179648 | tf_op jit(solution)/shard_map/all_gather | solution.py:277
  860.5 447.6 %all-gather.51.cloned.1.call-start = ((), (), s32[]{:S(2)}) async-start(), calls=%async_computation.36 | async-start | bytes 3538944 | tf_op jit(solution)/shard_map/all_gather | solution.py:277
  (82 other events, 260.9 us)
Sparse Core Ops, SparseCore 0:
  10.2 22.3 all-gather.38
  34.7 22.5 all-gather.40
  116.9 23.9 all-gather.42
  193.2 22.2 all-gather.44
  310.2 23.8 all-gather.46
  361.1 23.9 all-gather.48
  702.6 22.9 reduce-scatter.32
  728.7 27.9 reduce-scatter.28
  780.8 20.8 reduce-scatter.30
  807.5 27.1 reduce-scatter.26
  837.1 19.6 reduce-scatter.48
  859.1 19.5 reduce-scatter.44
  881.1 19.6 reduce-scatter.52
  903.1 19.6 reduce-scatter.50
  924.7 40.2 all-gather.56
  967.3 18.3 reduce-scatter.46
  988.5 19.6 reduce-scatter.42
  1011.2 31.1 reduce-scatter.40
  1044.9 31.1 reduce-scatter.38
  1079.0 31.1 reduce-scatter.36
  1112.7 31.1 reduce-scatter.34
  1146.1 60.0 all-gather.52
  1208.3 38.9 all-gather.54
  1249.3 58.7 all-gather.50
